TPU v7x, 32 devices: a whole 2x2x4 slice. The times are simulated.
32 devices in a mesh: dp: 8 (over z, y), tensor: 4 (over x, core).
Axes of the slice: x: 2, y: 2, z: 4, core: 2. Of those that a mesh axis runs over, the one named last changes fastest.
Arguments:
- pre_hidden: bfloat16 [8192, 2048], P(('dp', 'tensor')), may hold values from -6 to 6
- dec_hidden: bfloat16 [16, 2048], P('dp'), may hold values from -6 to 6
- norm_gain: bfloat16 [2048], replicated, may hold values from 0.5 to 1.5
- norm_shift: bfloat16 [2048], replicated, may hold values from -3 to 3
- qkv_weight: bfloat16 [2048, 6144], P(None, 'tensor'), may hold values from -0.125 to 0.125
- qkv_bias: bfloat16 [6144], P('tensor'), may hold values from -3 to 3
- out_weight: bfloat16 [2048, 2048], P('tensor'), may hold values from -0.125 to 0.125
- out_bias: bfloat16 [2048], replicated, may hold values from -3 to 3
- pre_keys: bfloat16 [8, 1024, 2048], P('dp', None, 'tensor'), may hold values from -480 to 480
- pre_values: bfloat16 [8, 1024, 2048], P('dp', None, 'tensor'), may hold values from -6 to 6
- dec_keys: bfloat16 [16, 2048, 2048], P('dp', None, 'tensor'), may hold values from -480 to 480
- dec_values: bfloat16 [16, 2048, 2048], P('dp', None, 'tensor'), may hold values from -6 to 6
- prefix_lengths: int32 [8], P('dp'), may hold values from 0 to 1024, as said below
- cache_lengths: int32 [16], P('dp'), may hold values from 1 to 2048, as said below
- slot_of: int32 [16], replicated, may hold values from 0 to 15, each once
Outputs:
- pre_output: bfloat16 [8192, 2048], P(('dp', 'tensor'))
- dec_output: bfloat16 [16, 2048], P('dp')
Inputs may be any that keep to these rules, and one draw needn't show every extreme that they name: `slot_of`: each decode slot is used by exactly one decode request. `prefix_lengths`: the longest prefix equals 1024. `cache_lengths`: the longest decode cache equals 2048.
All inputs are finite; a program needn't handle non-finite values.
Results may differ from a plain program's by a relative error of at most 0.0049.
The roundings to bfloat16 on the way count: a program that leaves them out, or rounds other values in their place, can miss the bound.
Values may be sent and summed in bfloat16 or wider, within the bound.
No kernel may reach another device: no remote copies, remote signals or barrier semaphores. Data moves between devices by JAX's collectives and lax.ppermute only.
A program may use at most 128 MiB of HBM per device.

v0:
```python
import math
import jax
import jax.numpy as jnp
from jax import lax
from jax.sharding import PartitionSpec as P

H = 16
HD = 128
EPSILON = 1e-05


def normalize(values, norm_gain, norm_shift):
    values = values.astype(jnp.float32)
    center = values - jnp.mean(values, axis=-1, keepdims=True)
    spread = jnp.mean(center * center, axis=-1, keepdims=True)
    scaled = center * lax.rsqrt(spread + EPSILON)
    return (scaled * norm_gain.astype(jnp.float32) + norm_shift.astype(jnp.float32)).astype(
        jnp.bfloat16
    )


def alibi_slopes(first_head, head_count, total_heads):
    head_ids = (first_head + jnp.arange(head_count, dtype=jnp.int32)).astype(jnp.float32)
    return jnp.exp2(-8.0 * (head_ids + 1.0) / total_heads)


def prefill_attention(merged_rows, cache_keys, cache_values, prefix, slopes):
    queries = merged_rows[:, :, 0]
    new_keys = merged_rows[:, :, 1]
    new_values = merged_rows[:, :, 2]
    group_size = merged_rows.shape[0]
    cache_size = cache_keys.shape[0]
    factor = 1.0 / math.sqrt(merged_rows.shape[-1])
    query_pos = prefix + jnp.arange(group_size, dtype=jnp.int32)
    cache_pos = jnp.arange(cache_size, dtype=jnp.int32)
    cache_dist = (query_pos[:, None] - cache_pos[None, :]).astype(jnp.float32)
    new_dist = (query_pos[:, None] - query_pos[None, :]).astype(jnp.float32)
    cache_scores = (
        jnp.einsum("qhd,khd->hqk", queries, cache_keys, preferred_element_type=jnp.float32) * factor
    )
    cache_scores = cache_scores - slopes[:, None, None] * cache_dist[None]
    cache_scores = jnp.where((cache_pos < prefix)[None, None, :], cache_scores, -jnp.inf)
    new_scores = (
        jnp.einsum("qhd,khd->hqk", queries, new_keys, preferred_element_type=jnp.float32) * factor
    )
    new_scores = new_scores - slopes[:, None, None] * new_dist[None]
    causal = (
        jnp.arange(group_size, dtype=jnp.int32)[None, :]
        <= jnp.arange(group_size, dtype=jnp.int32)[:, None]
    )
    new_scores = jnp.where(causal[None], new_scores, -jnp.inf)
    highest = jnp.maximum(
        jnp.max(cache_scores, axis=-1, keepdims=True), jnp.max(new_scores, axis=-1, keepdims=True)
    )
    cache_exp = jnp.exp(cache_scores - highest)
    new_exp = jnp.exp(new_scores - highest)
    denominator = jnp.sum(cache_exp, axis=-1, keepdims=True) + jnp.sum(
        new_exp, axis=-1, keepdims=True
    )
    cache_probs = (cache_exp / denominator).astype(jnp.bfloat16)
    new_probs = (new_exp / denominator).astype(jnp.bfloat16)
    context = jnp.einsum(
        "hqk,khd->qhd", cache_probs, cache_values, preferred_element_type=jnp.float32
    )
    context = context + jnp.einsum(
        "hqk,khd->qhd", new_probs, new_values, preferred_element_type=jnp.float32
    )
    return context.astype(jnp.bfloat16).reshape(group_size, -1)


def decode_attention(query_row, new_key, new_value, cache_keys, cache_values, length, slopes):
    factor = 1.0 / math.sqrt(query_row.shape[-1])
    cache_pos = jnp.arange(cache_keys.shape[0], dtype=jnp.int32)
    distance = (length - cache_pos).astype(jnp.float32)
    cache_scores = (
        jnp.einsum("hd,khd->hk", query_row, cache_keys, preferred_element_type=jnp.float32) * factor
    )
    cache_scores = cache_scores - slopes[:, None] * distance[None, :]
    cache_scores = jnp.where((cache_pos < length)[None, :], cache_scores, -jnp.inf)
    own_score = (
        jnp.einsum("hd,hd->h", query_row, new_key, preferred_element_type=jnp.float32)[:, None]
        * factor
    )
    highest = jnp.maximum(jnp.max(cache_scores, axis=-1, keepdims=True), own_score)
    cache_exp = jnp.exp(cache_scores - highest)
    own_exp = jnp.exp(own_score - highest)
    denominator = jnp.sum(cache_exp, axis=-1, keepdims=True) + own_exp
    cache_probs = (cache_exp / denominator).astype(jnp.bfloat16)
    own_prob = (own_exp / denominator).astype(jnp.bfloat16)
    context = jnp.einsum(
        "hk,khd->hd", cache_probs, cache_values, preferred_element_type=jnp.float32
    )
    context = context + own_prob.astype(jnp.float32) * new_value.astype(jnp.float32)
    return context.astype(jnp.bfloat16).reshape(-1)


def per_device(
    pre_hidden,
    dec_hidden,
    norm_gain,
    norm_shift,
    qkv_weight,
    qkv_bias,
    out_weight,
    out_bias,
    pre_keys,
    pre_values,
    dec_keys,
    dec_values,
    prefix_lengths,
    cache_lengths,
    slot_of,
):
    head_size = HD
    local_heads = qkv_weight.shape[1] // (3 * head_size)
    slopes = alibi_slopes(lax.axis_index("tensor") * local_heads, local_heads, H)
    bias_sum = out_bias.astype(jnp.float32)
    normed = normalize(pre_hidden, norm_gain, norm_shift)
    product = jnp.dot(
        lax.all_gather(normed, "tensor", axis=0, tiled=True),
        qkv_weight,
        preferred_element_type=jnp.float32,
    )
    merged_rows = (product + qkv_bias.astype(jnp.float32)).astype(jnp.bfloat16)
    group_size = merged_rows.shape[0]
    merged_rows = merged_rows.reshape(group_size, local_heads, 3, head_size)
    cache_size = pre_keys.shape[1]
    context = prefill_attention(
        merged_rows,
        pre_keys[0].reshape(cache_size, local_heads, head_size),
        pre_values[0].reshape(cache_size, local_heads, head_size),
        prefix_lengths[0],
        slopes,
    )
    summed = lax.psum_scatter(
        jnp.dot(context, out_weight, preferred_element_type=jnp.float32),
        "tensor",
        scatter_dimension=0,
        tiled=True,
    )
    pre_output = (summed + bias_sum + pre_hidden.astype(jnp.float32)).astype(jnp.bfloat16)
    slot_count = dec_hidden.shape[0]
    first_slot = lax.axis_index("dp") * slot_count
    slot_ids = first_slot + jnp.arange(slot_count, dtype=jnp.int32)
    request_ids = jnp.arange(slot_of.shape[0], dtype=jnp.int32)
    own_requests_slots = lax.dynamic_slice_in_dim(slot_of, first_slot, slot_count)
    to_slot = request_ids[:, None] == own_requests_slots[None, :]
    outgoing = jnp.zeros((slot_of.shape[0], dec_hidden.shape[1]), jnp.float32)
    for j in range(slot_count):
        outgoing = jnp.where(
            to_slot[:, j, None], dec_hidden[j][None, :].astype(jnp.float32), outgoing
        )
    arrived = lax.psum_scatter(outgoing, "dp", scatter_dimension=0, tiled=True).astype(jnp.bfloat16)
    normed_slots = normalize(arrived, norm_gain, norm_shift)
    merged_slots = (
        jnp.dot(normed_slots, qkv_weight, preferred_element_type=jnp.float32)
        + qkv_bias.astype(jnp.float32)
    ).astype(jnp.bfloat16)
    merged_slots = merged_slots.reshape(slot_count, local_heads, 3, head_size)
    dec_cache = dec_keys.shape[1]
    slot_context = jax.vmap(decode_attention, in_axes=(0, 0, 0, 0, 0, 0, None))(
        merged_slots[:, :, 0],
        merged_slots[:, :, 1],
        merged_slots[:, :, 2],
        dec_keys.reshape(slot_count, dec_cache, local_heads, head_size),
        dec_values.reshape(slot_count, dec_cache, local_heads, head_size),
        cache_lengths,
        slopes,
    )
    slot_partial = jnp.dot(slot_context, out_weight, preferred_element_type=jnp.float32)
    from_slot = slot_of[:, None] == slot_ids[None, :]
    returning = jnp.zeros((slot_of.shape[0], slot_partial.shape[1]), jnp.float32)
    for j in range(slot_count):
        returning = jnp.where(from_slot[:, j, None], slot_partial[j][None, :], returning)
    summed_all = lax.psum(returning, ("dp", "tensor"))
    slot_summed = lax.dynamic_slice_in_dim(summed_all, first_slot, slot_count)
    dec_output = (slot_summed + bias_sum + dec_hidden.astype(jnp.float32)).astype(jnp.bfloat16)
    return (pre_output, dec_output)


def solution(mesh):
    placed = (
        P(("dp", "tensor"), None),
        P("dp", None),
        P(),
        P(),
        P(None, "tensor"),
        P("tensor"),
        P("tensor", None),
        P(),
        P("dp", None, "tensor"),
        P("dp", None, "tensor"),
        P("dp", None, "tensor"),
        P("dp", None, "tensor"),
        P("dp"),
        P("dp"),
        P(),
    )
    return jax.shard_map(
        per_device,
        mesh=mesh,
        in_specs=placed,
        out_specs=(P(("dp", "tensor"), None), P("dp", None)),
        check_vma=False,
    )
```

profile of v0, /device:TPU:0, one launch (start us, length us, event | category | flops | bytes accessed | tf_op | source)
XLA Modules:
  0.0 232.2 jit_solution(11411439349456508695)
XLA Ops:
  8.1 0.8 convert_element_type.110
  8.9 0.7 convert_element_type.111
  9.6 1.4 convert_reduce_fusion
  11.1 1.6 fusion.10
  12.7 2.8 %fusion.13 = bf16[256,2048]{1,0:T(8,128)(2,1)} fusion(bf16[256,2048]{1,0:T(8,128)(2,1)} %param.15, f32[2048]{0:T(1024)S(1)} %convert_element_type.111, f32[2048]{0:T(1024)S(1)} %convert_element_type.110, f32[256]{0:T(256)S(1)} %add_rsqrt_fusion, f32[256]{0:T(256)S(1)} %broadcast_multiply_fusion), kind=kLoop, calls=%fused_computation.27 | loop fusion | flops 3145728 | bytes 2115584 | tf_op jit(solution)/shard_map/convert_element_type | solution.py:17
  15.8 40.1 %all-reduce.5 = bf16[16,2048]{1,0:T(8,128)(2,1)S(1)} all-reduce(f32[16,2048]{1,0:T(8,128)S(1)} %select_select_fusion.1), channel_id=3, replica_groups=mesh['dp'=8,'tensor'=4] {'dp'}, use_global_device_ids=true, to_apply=%region_7.8.clone | all-reduce | flops 32768 | bytes 196608
  56.0 0.6 dynamic-slice
  57.4 0.2 fusion.24
  57.6 3.8 %fusion.9 = bf16[2,1536]{1,0:T(2,128)(2,1)S(1)} fusion(bf16[2048,1536]{1,0:T(8,128)(2,1)} %param.19, bf16[2,2048]{1,0:T(2,128)(2,1)S(1)} %get-tuple-element.7, f32[2]{0:T(128)S(1)} %add_rsqrt_fusion.1, f32[2]{0:T(128)S(1)} %broadcast_multiply_fusion.1, f32[2048]{0:T(1024)S(1)} %convert_element_type.111, f32[2048]{0:T(1024)S(1)} %convert_element_type.110, ...), kind=kOutput, calls=%fused_computation.23 | convolution fusion | flops 12613632 | bytes 6328336 | tf_op jit(solution)/shard_map/dot_general | solution.py:156
  61.4 6.4 %copy.60 = bf16[2,2048,512]{1,2,0:T(8,128)(2,1)} copy(bf16[2,2048,512]{2,1,0:T(8,128)(2,1)} %param.25) | data formatting | bytes 8388608 | tf_op jit(solution)/shard_map/reshape | solution.py:165
  67.9 3.0 %fusion.34 = f32[2,4,1,2048]{3,2,1,0:T(1,128)S(1)} fusion(bf16[2,2048,4,128]{1,3,2,0:T(8,128)(2,1)} %bitcast.86, bf16[2,4,3,128]{3,2,1,0:T(4,128)(2,1)S(1)} %reshape.204), kind=kOutput, calls=%fused_computation.66 | convolution fusion | flops 4194304 | bytes 4263936 | tf_op jit(solution)/shard_map/vmap(hd,khd->hk)/dot_general | solution.py:76
  71.1 0.2 fusion.43
  71.3 0.2 fusion.20
  71.7 0.7 fusion.4
  72.4 0.4 fusion.37
  72.8 0.7 select_select_fusion
  73.6 1.3 iota_compare_fusion
  75.6 3.6 %subtract_convert_fusion = (f32[1024,1024]{0,1:T(8,128)}, f32[1024,1024]{0,1:T(8,128)}) fusion(s32[1024]{0:T(1024)S(1)} %iota_add_fusion), kind=kLoop, calls=%fused_computation.14 | loop fusion | flops 4194304 | bytes 8392704 | tf_op jit(solution)/shard_map/convert_element_type | solution.py:37
  79.1 1.3 reshape_squeeze.6
  80.5 2.3 copy.59
  82.8 11.2 %add_convert_fusion = bf16[1024,1536]{1,0:T(8,128)(2,1)} fusion(bf16[1024,2048]{1,0:T(8,128)(2,1)} %all-gather.2.cloned.1.call-done, bf16[2048,1536]{1,0:T(8,128)(2,1)} %param.19, f32[1536]{0:T(1024)S(1)} %convert_element_type.113), kind=kOutput, calls=%fused_computation.10 | convolution fusion | flops 6445596672 | bytes 13637632 | tf_op jit(solution)/shard_map/dot_general | solution.py:119
  94.0 4.7 %copy.40 = bf16[1024,1536]{0,1:T(8,128)(2,1)} copy(bf16[1024,1536]{1,0:T(8,128)(2,1)} %add_convert_fusion) | data formatting | bytes 6291456 | tf_op jit(solution)/shard_map/convert_element_type | solution.py:124
  98.7 10.9 %fusion.47 = (f32[4,1024]{1,0:T(4,128)S(1)}, f32[4,1024,1024]{1,2,0:T(8,128)}) fusion(f32[1024,1024]{0,1:T(8,128)} %get-tuple-element.15, f32[4]{0:T(128)S(1)} %multiply_exponential_fusion, bf16[1024,4,3,128]{0,3,2,1:T(8,128)(2,1)} %bitcast.87, pred[1024,1024]{0,1:T(8,128)(4,1)} %iota_compare_fusion), kind=kOutput, calls=%fused_computation.96 | convolution fusion | flops 1094709248 | bytes 24133648 | tf_op jit(solution)/shard_map/qhd,khd->hqk/dot_general | solution.py:44
  109.6 3.7 %fusion.46 = (f32[4,1024]{1,0:T(4,128)S(1)}, f32[4,1024,1024]{1,2,0:T(8,128)S(1)}) fusion(f32[1024,1024]{0,1:T(8,128)S(1)} %copy-done.1, f32[4]{0:T(128)S(1)} %multiply_exponential_fusion, bf16[1024,4,3,128]{0,3,2,1:T(8,128)(2,1)S(1)} %bitcast.88, bf16[1024,4,128]{2,1,0:T(4,128)(2,1)S(1)} %reshape_squeeze.6, pred[1024]{0:T(1024)(128)(4,1)S(1)} %iota_compare_fusion.2), kind=kOutput, calls=%fused_computation.95 | convolution fusion | flops 1094709248 | bytes 23086592 | tf_op jit(solution)/shard_map/qhd,khd->hqk/dot_general | solution.py:39
  113.3 8.4 %fusion.1 = (f32[4,1024]{1,0:T(4,128)S(1)}, f32[4,1024]{1,0:T(4,128)S(1)}) fusion(f32[4,1024,1024]{1,2,0:T(8,128)} %get-tuple-element.26, f32[4,1024]{1,0:T(4,128)S(1)} %max.12, f32[4,1024,1024]{1,2,0:T(8,128)S(1)} %get-tuple-element.24), kind=kLoop, calls=%fused_computation.7 | loop fusion | flops 16769024 | bytes 33603584 | tf_op jit(solution)/shard_map/reduce_sum | solution.py:57
  121.8 3.5 %fusion.2 = f32[4,1024,128]{1,2,0:T(8,128)S(1)} fusion(bf16[1024,4,128]{0,2,1:T(8,128)(2,1)S(1)} %bitcast.90, f32[4,1024,1024]{1,2,0:T(8,128)S(1)} %get-tuple-element.24, f32[4,1024]{1,0:T(4,128)S(1)} %add.158, f32[4,1024]{1,0:T(4,128)S(1)} %max.12), kind=kOutput, calls=%fused_computation.8 | convolution fusion | flops 1086324736 | bytes 19955712 | tf_op jit(solution)/shard_map/hqk,khd->qhd/dot_general | solution.py:62
  125.3 8.0 %fusion.15 = bf16[1024,4,128]{0,2,1:T(8,128)(2,1)S(1)} fusion(f32[4,1024,128]{1,2,0:T(8,128)S(1)} %fusion.2, f32[4,1024,1024]{1,2,0:T(8,128)} %get-tuple-element.26, f32[4,1024]{1,0:T(4,128)S(1)} %add.158, f32[4,1024]{1,0:T(4,128)S(1)} %max.12, bf16[1024,4,3,128]{0,3,2,1:T(8,128)(2,1)S(1)} %bitcast.89), kind=kOutput, calls=%fused_computation.30 | convolution fusion | flops 1087373312 | bytes 21004288 | tf_op jit(solution)/shard_map/hqk,khd->qhd/dot_general | solution.py:65
  133.2 5.6 %fusion.48 = f32[1024,2048]{1,0:T(8,128)} fusion(bf16[1024,512]{0,1:T(8,128)(2,1)S(1)} %bitcast.97, bf16[512,2048]{1,0:T(8,128)(2,1)S(1)} %copy-done), kind=kOutput, calls=%fused_computation.97 | convolution fusion | flops 2147483648 | bytes 11534336 | tf_op jit(solution)/shard_map/dot_general | solution.py:136
  138.9 0.7 copy-done.7
  139.5 80.9 %all-reduce.4.cloned.1.call-done = f32[16,2048]{1,0:T(8,128)} async-done(((f32[16,2048]{1,0:T(8,128)}), f32[16,2048]{1,0:T(8,128)}) %all-reduce.4.cloned.1.call-update) | async-done | bytes 131088 | tf_op jit(solution)/shard_map/psum | solution.py:175
  220.4 1.5 add_convert_fusion.1
  221.8 2.9 %fusion.14 = bf16[256,2048]{1,0:T(8,128)(2,1)} fusion(bf16[256,2048]{1,0:T(8,128)(2,1)S(1)} %copy-done.2, f32[256,2048]{1,0:T(8,128)} %reduce-scatter.2.cloned.1.call-done, f32[2048]{0:T(1024)S(1)} %convert_element_type.121), kind=kLoop, calls=%fused_computation.28 | loop fusion | flops 2097152 | bytes 4202496 | tf_op jit(solution)/shard_map/convert_element_type | solution.py:141
  (61 shorter events, 1.3 us)
Async XLA Ops:
  8.0 64.4 %copy-start = (bf16[512,2048]{1,0:T(8,128)(2,1)S(1)}, bf16[512,2048]{1,0:T(8,128)(2,1)}, u32[]{:S(2)}) copy-start(bf16[512,2048]{1,0:T(8,128)(2,1)} %param.21) | copy-start | bytes 6291460
  8.0 48.0 %copy-start.11 = (u32[32]{0:T(128)S(1)}, u32[32]{0:T(128)}, u32[]{:S(2)}) copy-start(u32[32]{0:T(128)} %constant.56) | copy-start | bytes 388
  8.0 7.5 %copy-start.10 = (s32[16]{0:T(128)S(1)}, s32[16]{0:T(128)}, u32[]{:S(2)}) copy-start(s32[16]{0:T(128)} %param.29) | copy-start | bytes 196
  8.0 7.7 %copy-start.5 = (bf16[2,2048]{1,0:T(2,128)(2,1)S(1)}, bf16[2,2048]{1,0:T(2,128)(2,1)}, u32[]{:S(2)}) copy-start(bf16[2,2048]{1,0:T(2,128)(2,1)} %param.16) | copy-start | bytes 24580
  8.0 47.9 %copy-start.6 = (bf16[1536]{0:T(1024)(128)(2,1)S(1)}, bf16[1536]{0:T(1024)(128)(2,1)}, u32[]{:S(2)}) copy-start(bf16[1536]{0:T(1024)(128)(2,1)} %param.20) | copy-start | bytes 9220
  8.1 74.7 %all-gather.2.cloned.1.call-start = ((), (), s32[]{:S(2)}) async-start(), calls=%async_computation.1 | async-start | bytes 5242880 | tf_op jit(solution)/shard_map/all_gather | solution.py:120
  15.5 204.9 %all-reduce.4.cloned.1.call-start = ((), (), s32[]{:S(2)}) async-start(), calls=%async_computation.3 | async-start | bytes 262144 | tf_op jit(solution)/shard_map/psum | solution.py:175
  67.8 3.1 %copy-start.8 = (s32[2]{0:T(128)S(1)}, s32[2]{0:T(128)}, u32[]{:S(2)}) copy-start(s32[2]{0:T(128)} %param.28) | copy-start | bytes 28
  67.8 3.9 %copy-start.9 = (bf16[2,2048,512]{2,1,0:T(8,128)(2,1)S(1)}, bf16[2,2048,512]{2,1,0:T(8,128)(2,1)}, u32[]{:S(2)}) copy-start(bf16[2,2048,512]{2,1,0:T(8,128)(2,1)} %param.26) | copy-start | bytes 12582916
  73.6 148.3 %reduce-scatter.2.cloned.1.call-start = ((), (), s32[]{:S(2)}) async-start(), calls=%async_computation.2 | async-start | bytes 10485760 | tf_op jit(solution)/shard_map/reduce_scatter | solution.py:135
  98.7 10.9 %copy-start.1 = (f32[1024,1024]{0,1:T(8,128)S(1)}, f32[1024,1024]{0,1:T(8,128)}, u32[]{:S(2)}) copy-start(f32[1024,1024]{0,1:T(8,128)} %get-tuple-element.16) | copy-start | bytes 12582916
  98.7 10.9 %copy-start.3 = (bf16[1024,1536]{0,1:T(8,128)(2,1)S(1)}, bf16[1024,1536]{0,1:T(8,128)(2,1)}, u32[]{:S(2)}) copy-start(bf16[1024,1536]{0,1:T(8,128)(2,1)} %copy.40) | copy-start | bytes 9437188
  113.3 8.5 %copy-start.4 = (bf16[1,1024,512]{1,2,0:T(8,128)(2,1)S(1)}, bf16[1,1024,512]{1,2,0:T(8,128)(2,1)}, u32[]{:S(2)}) copy-start(bf16[1,1024,512]{1,2,0:T(8,128)(2,1)} %copy.59) | copy-start | bytes 3145732
  138.8 0.7 copy-start.7
  138.8 83.0 %copy-start.2 = (bf16[256,2048]{1,0:T(8,128)(2,1)S(1)}, bf16[256,2048]{1,0:T(8,128)(2,1)}, u32[]{:S(2)}) copy-start(bf16[256,2048]{1,0:T(8,128)(2,1)} %param.15) | copy-start | bytes 3145732
Sparse Core Ops, SparseCore 0:
  15.6 37.1 all-gather.1
  139.0 69.1 reduce-scatter.1
Sparse Core Ops, SparseCore 1:
  73.6 146.7 all-reduce.3
where the time goes:
time: 233 us; the launch traced here: 232 us
  waiting for transfers between devices  80.9 us (35%)
  matrix products  50.6 us (22%)
  blocking collectives  40.1 us (17%)
  other arithmetic  27.2 us (12%)
  between operations  17.1 us (7%)
  local copies, waits for them, and re-layouts  16.2 us (7%)
    psum x1, waiting for transfers between devices, per_device(): summed_all = lax.psum(returning, ('dp', 'tensor'))  80.9 us
    unnamed x1, blocking collectives  40.1 us
    dot_general x1, matrix products, per_device(): jnp.dot(lax.all_gather(normed, 'tensor', axis=0, tiled=True), qkv_weight,...  11.2 us
    dot_general x1, matrix products, prefill_attention(): jnp.einsum('qhd,khd->hqk', queries, new_keys, preferred_element_type=jnp....  10.9 us
    reduce_sum x1, other arithmetic, prefill_attention(): jnp.sum(new_exp, axis=-1, keepdims=True)  8.43 us
    dot_general x1, matrix products, prefill_attention(): jnp.einsum('hqk,khd->qhd', new_probs, new_values, preferred_element_type=...  7.95 us
    reshape x1, local copies, waits for them, and re-layouts, per_device(): dec_keys.reshape(slot_count, dec_cache, local_heads, head_size)  6.41 us
    dot_general x1, matrix products, per_device(): jnp.dot(context, out_weight, preferred_element_type=jnp.float32)  5.61 us
  transfers between devices with their start and end apart: 3, of which 1 were waited for; matrix products, arithmetic and copies ran while one was open for 36% of the time, Pallas kernels for 0%

commit v1 on v0

--- a/solution.py
+++ b/solution.py
@@ -172,7 +172,9 @@
     returning = jnp.zeros((slot_of.shape[0], slot_partial.shape[1]), jnp.float32)
     for j in range(slot_count):
         returning = jnp.where(from_slot[:, j, None], slot_partial[j][None, :], returning)
-    summed_all = lax.psum(returning, ("dp", "tensor"))
+    summed_all = returning
+    for mesh_axis in ("tensor", "dp"):
+        summed_all = lax.psum(summed_all, mesh_axis)
     slot_summed = lax.dynamic_slice_in_dim(summed_all, first_slot, slot_count)
     dec_output = (slot_summed + bias_sum + dec_hidden.astype(jnp.float32)).astype(jnp.bfloat16)
     return (pre_output, dec_output)

time: 233 us -> 295 us (1.27)
  waiting for transfers between devices: 80.9 us -> 139 us
  matrix products: 50.6 us -> 54.7 us
    reduce_scatter x1, waiting for transfers between devices: 0.01 us -> 72 us  [per_device(): lax.psum_scatter(jnp.dot(context, out_weight, preferred_element_type=jnp....]
    psum x1 -> x2, waiting for transfers between devices: 80.9 us -> 31 us  [per_device(): summed_all = lax.psum(summed_all, mesh_axis)]
    all_gather x1, waiting for transfers between devices: 0.01 us -> 35.9 us  [per_device(): lax.all_gather(normed, 'tensor', axis=0, tiled=True)]
  transfers between devices with their start and end apart: 3 -> 4, of which waited for: 1 -> 4; matrix products, arithmetic and copies ran while one was open for 36% -> 24% of each run, Pallas kernels for 0% -> 0%
where the time goes in v1:
time: 295 us; the launch traced here: 294 us
  waiting for transfers between devices  139 us (47%)
  matrix products  54.7 us (19%)
  blocking collectives  40.2 us (14%)
  other arithmetic  26.4 us (9%)
  local copies, waits for them, and re-layouts  18.1 us (6%)
  between operations  15.3 us (5%)
    reduce_scatter x1, waiting for transfers between devices, per_device(): lax.psum_scatter(jnp.dot(context, out_weight, preferred_element_type=jnp....  72 us
    unnamed x1, blocking collectives  40.2 us
    all_gather x1, waiting for transfers between devices, per_device(): lax.all_gather(normed, 'tensor', axis=0, tiled=True)  35.9 us
    psum x2, waiting for transfers between devices, per_device(): summed_all = lax.psum(summed_all, mesh_axis)  31 us
    dot_general x1, matrix products, per_device(): jnp.dot(lax.all_gather(normed, 'tensor', axis=0, tiled=True), qkv_weight,...  11.2 us
    dot_general x1, matrix products, prefill_attention(): jnp.einsum('qhd,khd->hqk', queries, new_keys, preferred_element_type=jnp....  10.9 us
    reduce_sum x1, other arithmetic, prefill_attention(): jnp.sum(new_exp, axis=-1, keepdims=True)  8.44 us
    dot_general x1, matrix products, prefill_attention(): jnp.einsum('hqk,khd->qhd', new_probs, new_values, preferred_element_type=...  8.27 us
  transfers between devices with their start and end apart: 4, of which 4 were waited for; matrix products, arithmetic and copies ran while one was open for 24% of the time, Pallas kernels for 0%

profile of v1, /device:TPU:0, one launch (start us, length us, event | category | flops | bytes accessed | tf_op | source)
XLA Modules:
  0.0 294.0 jit_solution(7164739672589543817)
XLA Ops:
  7.2 0.9 subtract_convert_fusion.2
  8.1 0.7 iota_compare_fusion.1
  8.9 0.7 dynamic_slice.6
  9.7 0.8 slice_convert_fusion.1
  10.6 40.2 %all-reduce.8 = bf16[16,2048]{1,0:T(8,128)(2,1)S(1)} all-reduce(f32[16,2048]{1,0:T(8,128)S(1)} %select_select_fusion.1), channel_id=3, replica_groups=mesh['dp'=8,'tensor'=4] {'dp'}, use_global_device_ids=true, to_apply=%region_7.8.clone | all-reduce | flops 32768 | bytes 196608
  50.8 1.2 dynamic-slice
  53.0 0.7 convert_element_type.110
  53.7 0.7 convert_element_type.111
  55.1 3.7 %fusion.9 = bf16[2,1536]{1,0:T(2,128)(2,1)S(1)} fusion(bf16[2048,1536]{1,0:T(8,128)(2,1)} %param.19, bf16[2,2048]{1,0:T(2,128)(2,1)S(1)} %get-tuple-element.7, f32[2]{0:T(128)S(1)} %add_rsqrt_fusion.1, f32[2]{0:T(128)S(1)} %broadcast_multiply_fusion.1, f32[2048]{0:T(1024)S(1)} %convert_element_type.111, f32[2048]{0:T(1024)S(1)} %convert_element_type.110, ...), kind=kOutput, calls=%fused_computation.23 | convolution fusion | flops 12613632 | bytes 6328336 | tf_op jit(solution)/shard_map/dot_general | solution.py:156
  58.9 6.3 %copy.60 = bf16[2,2048,512]{1,2,0:T(8,128)(2,1)} copy(bf16[2,2048,512]{2,1,0:T(8,128)(2,1)} %param.25) | data formatting | bytes 8388608 | tf_op jit(solution)/shard_map/reshape | solution.py:165
  65.2 2.8 fusion.34
  68.6 2.8 fusion.4
  72.1 0.7 select_select_fusion
  73.6 1.5 fusion.13
  75.8 2.1 reshape_squeeze.6
  78.0 2.3 copy.59
  80.2 1.4 iota_compare_fusion
  81.6 3.6 %subtract_convert_fusion = (f32[1024,1024]{0,1:T(8,128)}, f32[1024,1024]{0,1:T(8,128)}) fusion(s32[1024]{0:T(1024)S(1)} %iota_add_fusion), kind=kLoop, calls=%fused_computation.14 | loop fusion | flops 4194304 | bytes 8392704 | tf_op jit(solution)/shard_map/convert_element_type | solution.py:37
  85.2 16.5 %all-reduce.5.cloned.1.call-done = f32[16,2048]{1,0:T(8,128)} async-done(((f32[16,2048]{1,0:T(8,128)}), f32[16,2048]{1,0:T(8,128)}) %all-reduce.5.cloned.1.call-update) | async-done | bytes 131088 | tf_op jit(solution)/shard_map/psum | solution.py:177
  101.9 35.9 %all-gather.2.cloned.1.call-done = bf16[1024,2048]{1,0:T(8,128)(2,1)} async-done(((bf16[256,2048]{1,0:T(8,128)(2,1)}), bf16[1024,2048]{1,0:T(8,128)(2,1)}) %all-gather.2.cloned.1.call-update) | async-done | bytes 4194320 | tf_op jit(solution)/shard_map/all_gather | solution.py:120
  137.8 11.2 %add_convert_fusion = bf16[1024,1536]{1,0:T(8,128)(2,1)} fusion(bf16[1024,2048]{1,0:T(8,128)(2,1)} %all-gather.2.cloned.1.call-done, bf16[2048,1536]{1,0:T(8,128)(2,1)} %param.19, f32[1536]{0:T(1024)S(1)} %convert_element_type.113), kind=kOutput, calls=%fused_computation.10 | convolution fusion | flops 6445596672 | bytes 13637632 | tf_op jit(solution)/shard_map/dot_general | solution.py:119
  149.0 4.7 %copy.40 = bf16[1024,1536]{0,1:T(8,128)(2,1)} copy(bf16[1024,1536]{1,0:T(8,128)(2,1)} %add_convert_fusion) | data formatting | bytes 6291456 | tf_op jit(solution)/shard_map/convert_element_type | solution.py:124
  153.7 10.9 %fusion.47 = (f32[4,1024]{1,0:T(4,128)S(1)}, f32[4,1024,1024]{1,2,0:T(8,128)}) fusion(f32[1024,1024]{0,1:T(8,128)} %get-tuple-element.15, f32[4]{0:T(128)S(1)} %multiply_exponential_fusion, bf16[1024,4,3,128]{0,3,2,1:T(8,128)(2,1)} %bitcast.87, pred[1024,1024]{0,1:T(8,128)(4,1)} %iota_compare_fusion), kind=kOutput, calls=%fused_computation.96 | convolution fusion | flops 1094709248 | bytes 24133648 | tf_op jit(solution)/shard_map/qhd,khd->hqk/dot_general | solution.py:44
  164.7 4.6 %fusion.46 = (f32[4,1024]{1,0:T(4,128)S(1)}, f32[4,1024,1024]{1,2,0:T(8,128)S(1)}) fusion(f32[1024,1024]{0,1:T(8,128)S(1)} %copy-done.1, f32[4]{0:T(128)S(1)} %multiply_exponential_fusion, bf16[1024,4,3,128]{0,3,2,1:T(8,128)(2,1)S(1)} %bitcast.88, bf16[1024,4,128]{2,1,0:T(4,128)(2,1)} %reshape_squeeze.6, pred[1024]{0:T(1024)(128)(4,1)S(1)} %iota_compare_fusion.2), kind=kOutput, calls=%fused_computation.95 | convolution fusion | flops 1094709248 | bytes 23086592 | tf_op jit(solution)/shard_map/qhd,khd->hqk/dot_general | solution.py:39
  169.3 8.4 %fusion.1 = (f32[4,1024]{1,0:T(4,128)S(1)}, f32[4,1024]{1,0:T(4,128)S(1)}) fusion(f32[4,1024,1024]{1,2,0:T(8,128)} %get-tuple-element.26, f32[4,1024]{1,0:T(4,128)S(1)} %max.12, f32[4,1024,1024]{1,2,0:T(8,128)S(1)} %get-tuple-element.24), kind=kLoop, calls=%fused_computation.7 | loop fusion | flops 16769024 | bytes 33603584 | tf_op jit(solution)/shard_map/reduce_sum | solution.py:57
  177.8 4.3 %fusion.2 = f32[4,1024,128]{1,2,0:T(8,128)} fusion(bf16[1024,4,128]{0,2,1:T(8,128)(2,1)S(1)} %bitcast.90, f32[4,1024,1024]{1,2,0:T(8,128)S(1)} %get-tuple-element.24, f32[4,1024]{1,0:T(4,128)S(1)} %add.160, f32[4,1024]{1,0:T(4,128)S(1)} %max.12), kind=kOutput, calls=%fused_computation.8 | convolution fusion | flops 1086324736 | bytes 19955712 | tf_op jit(solution)/shard_map/hqk,khd->qhd/dot_general | solution.py:62
  182.1 8.3 %fusion.15 = bf16[1024,4,128]{0,2,1:T(8,128)(2,1)S(1)} fusion(f32[4,1024,128]{1,2,0:T(8,128)} %fusion.2, f32[4,1024,1024]{1,2,0:T(8,128)} %get-tuple-element.26, f32[4,1024]{1,0:T(4,128)S(1)} %add.160, f32[4,1024]{1,0:T(4,128)S(1)} %max.12, bf16[1024,4,3,128]{0,3,2,1:T(8,128)(2,1)S(1)} %bitcast.89), kind=kOutput, calls=%fused_computation.30 | convolution fusion | flops 1087373312 | bytes 21004288 | tf_op jit(solution)/shard_map/hqk,khd->qhd/dot_general | solution.py:65
  190.4 5.6 %fusion.48 = f32[1024,2048]{1,0:T(8,128)} fusion(bf16[1024,512]{0,1:T(8,128)(2,1)S(1)} %bitcast.97, bf16[512,2048]{1,0:T(8,128)(2,1)S(1)} %copy-done), kind=kOutput, calls=%fused_computation.97 | convolution fusion | flops 2147483648 | bytes 11534336 | tf_op jit(solution)/shard_map/dot_general | solution.py:136
  196.7 14.5 %all-reduce.7.cloned.1.call-done = f32[16,2048]{1,0:T(8,128)} async-done(((f32[16,2048]{1,0:T(8,128)}), f32[16,2048]{1,0:T(8,128)}) %all-reduce.7.cloned.1.call-update) | async-done | bytes 131088 | tf_op jit(solution)/shard_map/psum | solution.py:177
  211.2 1.5 add_convert_fusion.1
  212.6 72.0 %reduce-scatter.2.cloned.1.call-done = f32[256,2048]{1,0:T(8,128)} async-done(((f32[1024,2048]{1,0:T(8,128)}), f32[256,2048]{1,0:T(8,128)}) %reduce-scatter.2.cloned.1.call-update) | async-done | bytes 2097168 | tf_op jit(solution)/shard_map/reduce_scatter | solution.py:135
  284.6 2.9 fusion.14
  (56 shorter events, 4.2 us)
Async XLA Ops:
  7.2 64.4 %copy-start = (bf16[512,2048]{1,0:T(8,128)(2,1)S(1)}, bf16[512,2048]{1,0:T(8,128)(2,1)}, u32[]{:S(2)}) copy-start(bf16[512,2048]{1,0:T(8,128)(2,1)} %param.21) | copy-start | bytes 6291460
  7.2 94.5 %all-reduce.5.cloned.1.call-start = ((), (), s32[]{:S(2)}) async-start(), calls=%async_computation.3 | async-start | bytes 262144 | tf_op jit(solution)/shard_map/psum | solution.py:177
  68.0 4.0 %copy-start.7 = (s32[16]{0:T(128)S(1)}, s32[16]{0:T(128)}, u32[]{:S(2)}) copy-start(s32[16]{0:T(128)} %param.29) | copy-start | bytes 196
  68.0 4.9 %copy-start.2 = (bf16[256,2048]{1,0:T(8,128)(2,1)S(1)}, bf16[256,2048]{1,0:T(8,128)(2,1)}, u32[]{:S(2)}) copy-start(bf16[256,2048]{1,0:T(8,128)(2,1)} %param.15) | copy-start | bytes 3145732
  72.8 65.0 %all-gather.2.cloned.1.call-start = ((), (), s32[]{:S(2)}) async-start(), calls=%async_computation.1 | async-start | bytes 5242880 | tf_op jit(solution)/shard_map/all_gather | solution.py:120
  75.1 136.0 %all-reduce.7.cloned.1.call-start = ((), (), s32[]{:S(2)}) async-start(), calls=%async_computation.4 | async-start | bytes 262144 | tf_op jit(solution)/shard_map/psum | solution.py:177
  101.7 182.9 %reduce-scatter.2.cloned.1.call-start = ((), (), s32[]{:S(2)}) async-start(), calls=%async_computation.2 | async-start | bytes 10485760 | tf_op jit(solution)/shard_map/reduce_scatter | solution.py:135
  153.7 10.9 %copy-start.1 = (f32[1024,1024]{0,1:T(8,128)S(1)}, f32[1024,1024]{0,1:T(8,128)}, u32[]{:S(2)}) copy-start(f32[1024,1024]{0,1:T(8,128)} %get-tuple-element.16) | copy-start | bytes 12582916
  153.7 10.9 %copy-start.3 = (bf16[1024,1536]{0,1:T(8,128)(2,1)S(1)}, bf16[1024,1536]{0,1:T(8,128)(2,1)}, u32[]{:S(2)}) copy-start(bf16[1024,1536]{0,1:T(8,128)(2,1)} %copy.40) | copy-start | bytes 9437188
  169.3 8.5 %copy-start.4 = (bf16[1,1024,512]{1,2,0:T(8,128)(2,1)S(1)}, bf16[1,1024,512]{1,2,0:T(8,128)(2,1)}, u32[]{:S(2)}) copy-start(bf16[1,1024,512]{1,2,0:T(8,128)(2,1)} %copy.59) | copy-start | bytes 3145732
  196.0 0.7 copy-start.6
  196.0 15.2 %copy-start.5 = (bf16[2,2048]{1,0:T(2,128)(2,1)S(1)}, bf16[2,2048]{1,0:T(2,128)(2,1)}, u32[]{:S(2)}) copy-start(bf16[2,2048]{1,0:T(2,128)(2,1)} %param.16) | copy-start | bytes 24580
Sparse Core Ops, SparseCore 0:
  73.0 28.6 all-reduce.4
  103.3 34.4 all-gather.1
  141.5 69.5 all-reduce.6
  213.6 70.9 reduce-scatter.1
